TPU v7x, 512 devices: a whole 4x4x16 slice. The times are simulated.
512 devices in a mesh: vox: 32 (over y, x, core), tm: 16 (over z).
Axes of the slice: x: 4, y: 4, z: 16, core: 2. Of those that a mesh axis runs over, the one named last changes fastest.
Arguments:
- series: float32 [2048, 65536], P('tm', 'vox'), may hold values from -40 to 40
- spikes: int32 [2048, 65536], P('tm', 'vox'), may hold values from 0 to 15
- motion: float32 [2048, 6], P('tm'), may hold values from -5 to 5
- tissue: float32 [3, 65536], P(None, 'vox'), may hold values from 0.01 to 12, as said below
Outputs:
- cleaned: float32 [2048, 65536], P('tm', 'vox')
Inputs may be any that keep to these rules, and one draw needn't show every extreme that they name: Bit j-1 of an entry (spikes // 2^(j-1) odd) flags that frame's level-j coefficient of that voxel as a spike. `tissue`: all weights are positive.
All inputs are finite; a program needn't handle non-finite values.
Results may differ from a plain program's by a relative error of at most 0.0003.
Values sent between devices are 32-bit elements; how exact they have to be, the bound alone decides.
No kernel may reach another device: no remote copies, remote signals or barrier semaphores. Data moves between devices by JAX's collectives and lax.ppermute only.
A program may use at most 64 MiB of HBM per device.

v0:
```python
import jax
import jax.numpy as jnp
from jax import lax
from jax.sharding import PartitionSpec as P

LEVELS = 4


def from_behind(block, axis, distance):
    devices = range(lax.axis_size(axis))
    route = [((i - distance) % len(devices), i) for i in devices]
    return lax.ppermute(block, axis, route)


def shifted(block, axis, distance):
    devices = range(lax.axis_size(axis))
    route = [(i - distance, i) for i in devices if i - distance in devices]
    return lax.ppermute(block, axis, route)


def precise_product(left, right):
    return jnp.dot(left, right, precision=lax.Precision.HIGHEST, preferred_element_type=jnp.float32)


def keep_level(spikes, level):
    return 1.0 - (spikes // 2**level % 2).astype(jnp.float32)


def despike_levelwise(series, spikes):
    frames = series.shape[0]
    approx = series
    kept_list = []
    for level in range(LEVELS):
        shift_rows = 2**level
        earlier = from_behind(approx[frames - shift_rows :], "tm", 1)
        lagged = jnp.concatenate([earlier, approx[: frames - shift_rows]], axis=0)
        detail = (approx - lagged) * 0.5
        kept_list.append(detail * keep_level(spikes, level))
        approx = (approx + lagged) * 0.5
    for level in range(LEVELS - 1, -1, -1):
        shift_rows = 2**level
        kept = kept_list[level]
        heads = from_behind(jnp.stack([approx[:shift_rows], kept[:shift_rows]]), "tm", -1)
        lead_approx = jnp.concatenate([approx[shift_rows:], heads[0]], axis=0)
        lead_kept = jnp.concatenate([kept[shift_rows:], heads[1]], axis=0)
        approx = (approx + lead_approx) * 0.5 + (kept - lead_kept) * 0.5
    return approx


def local(series, spikes, motion, tissue):
    spike_free_series = despike_levelwise(series, spikes)
    numer = precise_product(spike_free_series, tissue.T)
    numer = lax.psum(numer, "vox")
    voxel_signals = numer / float(tissue.shape[1] * lax.axis_size("vox"))
    base_regressors = jnp.concatenate([motion, voxel_signals], axis=1)
    previous_frames = shifted(base_regressors[base_regressors.shape[0] - 1 :], "tm", 1)
    before = jnp.concatenate([previous_frames, base_regressors[:-1]], axis=0)
    temporal_derivative = base_regressors - before
    nuisance_matrix = jnp.concatenate(
        [
            base_regressors,
            temporal_derivative,
            base_regressors * base_regressors,
            temporal_derivative * temporal_derivative,
        ],
        axis=1,
    )
    gram_matrix = precise_product(nuisance_matrix.T, nuisance_matrix)
    cross_products = precise_product(nuisance_matrix.T, spike_free_series)
    gram_matrix, cross_products = lax.psum((gram_matrix, cross_products), "tm")
    factor = jnp.linalg.cholesky(gram_matrix)
    beta_estimates = jax.scipy.linalg.cho_solve((factor, True), cross_products)
    return spike_free_series - precise_product(nuisance_matrix, beta_estimates)


def solution(mesh):
    return jax.shard_map(
        local,
        mesh=mesh,
        in_specs=(P("tm", "vox"), P("tm", "vox"), P("tm", None), P(None, "vox")),
        out_specs=P("tm", "vox"),
        check_vma=False,
    )
```

profile of v0, /device:TPU:2, one launch (start us, length us, event | category | flops | bytes accessed | tf_op | source)
XLA Modules:
  0.0 347.5 jit_solution(11441887220270911308)
XLA Ops:
  6.5 0.9 slice.120
  7.4 3.8 %collective-permute-start = (f32[1,2048]{1,0:T(1,128)S(1)}, f32[1,2048]{1,0:T(1,128)S(1)}, u32[]{:S(2)}, u32[]{:S(2)}) collective-permute-start(f32[1,2048]{1,0:T(1,128)S(1)} %slice.120), channel_id=1, source_target_pairs={{15,0},{0,1},{1,2},{2,3},{3,4},{4,5},{5,6},{6,7},{7,8},{8,9},{9,10... | collective-permute-start | bytes 24584 | tf_op jit(solution)/shard_map/ppermute | solution.py:12
  11.2 9.2 %collective-permute-done = f32[1,2048]{1,0:T(1,128)S(1)} collective-permute-done((f32[1,2048]{1,0:T(1,128)S(1)}, f32[1,2048]{1,0:T(1,128)S(1)}, u32[]{:S(2)}, u32[]{:S(2)}) %collective-permute-start) | collective-permute-done | bytes 8224 | tf_op jit(solution)/shard_map/ppermute | solution.py:12
  20.4 2.6 fusion.16
  23.1 1.9 collective-permute-start.1
  25.0 4.9 %collective-permute-done.1 = f32[2,2048]{1,0:T(2,128)S(1)} collective-permute-done((f32[2,2048]{1,0:T(2,128)S(1)}, f32[2,2048]{1,0:T(2,128)S(1)}, u32[]{:S(2)}, u32[]{:S(2)}) %collective-permute-start.1) | collective-permute-done | bytes 16416 | tf_op jit(solution)/shard_map/ppermute | solution.py:12
  29.9 1.3 fusion.13
  31.2 1.9 collective-permute-start.2
  33.1 5.1 %collective-permute-done.2 = f32[4,2048]{1,0:T(4,128)S(1)} collective-permute-done((f32[4,2048]{1,0:T(4,128)S(1)}, f32[4,2048]{1,0:T(4,128)S(1)}, u32[]{:S(2)}, u32[]{:S(2)}) %collective-permute-start.2) | collective-permute-done | bytes 32800 | tf_op jit(solution)/shard_map/ppermute | solution.py:12
  38.2 1.3 fusion.9
  39.5 1.9 collective-permute-start.3
  41.5 5.3 %collective-permute-done.3 = f32[8,2048]{1,0:T(8,128)S(1)} collective-permute-done((f32[8,2048]{1,0:T(8,128)S(1)}, f32[8,2048]{1,0:T(8,128)S(1)}, u32[]{:S(2)}, u32[]{:S(2)}) %collective-permute-start.3) | collective-permute-done | bytes 65568 | tf_op jit(solution)/shard_map/ppermute | solution.py:12
  46.9 1.2 fusion.4
  48.1 1.9 collective-permute-start.4
  50.2 5.4 %collective-permute-done.4 = f32[2,8,2048]{2,1,0:T(8,128)S(1)} collective-permute-done((f32[2,8,2048]{2,1,0:T(8,128)S(1)}, f32[2,8,2048]{2,1,0:T(8,128)S(1)}, u32[]{:S(2)}, u32[]{:S(2)}) %collective-permute-start.4) | collective-permute-done | bytes 131104 | tf_op jit(solution)/shard_map/ppermute | solution.py:12
  56.1 2.4 collective-permute-start.5
  58.7 3.5 %collective-permute-done.5 = f32[2,4,2048]{2,1,0:T(4,128)S(1)} collective-permute-done((f32[2,4,2048]{2,1,0:T(4,128)S(1)}, f32[2,4,2048]{2,1,0:T(4,128)S(1)}, u32[]{:S(2)}, u32[]{:S(2)}) %collective-permute-start.5) | collective-permute-done | bytes 65568 | tf_op jit(solution)/shard_map/ppermute | solution.py:12
  62.6 4.0 %collective-permute-start.6 = (f32[2,2,2048]{2,1,0:T(2,128)S(1)}, f32[2,2,2048]{2,1,0:T(2,128)S(1)}, u32[]{:S(2)}, u32[]{:S(2)}) collective-permute-start(f32[2,2,2048]{2,1,0:T(2,128)S(1)} %pad_maximum_fusion.6), channel_id=1, source_target_pairs={{1,0},{2,1},{3,2},{4,3},{5,4},{6,5},{7,6},{8,7},{9,8},{10,9},{11,1... | collective-permute-start | bytes 98312 | tf_op jit(solution)/shard_map/ppermute | solution.py:12
  66.8 1.6 collective-permute-done.6
  68.8 5.2 %collective-permute-start.7 = (f32[2,1,2048]{2,1,0:T(1,128)S(1)}, f32[2,1,2048]{2,1,0:T(1,128)S(1)}, u32[]{:S(2)}, u32[]{:S(2)}) collective-permute-start(f32[2,1,2048]{2,1,0:T(1,128)S(1)} %pad_maximum_fusion.7), channel_id=1, source_target_pairs={{1,0},{2,1},{3,2},{4,3},{5,4},{6,5},{7,6},{8,7},{9,8},{10,9},{11,1... | collective-permute-start | bytes 49160 | tf_op jit(solution)/shard_map/ppermute | solution.py:12
  74.2 1.2 collective-permute-done.7
  75.8 0.9 fusion.38
  76.7 57.6 %psum.21 = f32[128,3]{0,1:T(4,128)S(1)} all-reduce(f32[128,3]{0,1:T(4,128)S(1)} %fusion.38), channel_id=1, replica_groups=mesh['vox'=32,'tm'=16] {'vox'}, use_global_device_ids=true, to_apply=%region_0.1 | all-reduce | flops 384 | bytes 3072 | tf_op jit(solution)/shard_map/psum | solution.py:53
  134.4 1.3 collective-permute-start.8
  135.7 1.3 collective-permute-done.8
  137.7 1.4 fusion.40
  139.1 58.9 %psum.22 = f32[36,36]{0,1:T(8,128)S(1)} all-reduce(f32[36,36]{0,1:T(8,128)S(1)} %fusion.39), channel_id=1, replica_groups=mesh['vox'=32,'tm'=16] {'tm'}, use_global_device_ids=true, to_apply=%region_1.2 | all-reduce | flops 1296 | bytes 10368 | tf_op jit(solution)/shard_map/psum | solution.py:70
  198.1 3.3 cholesky.16
  202.8 2.8 custom-call.10
  205.5 131.3 %all-reduce.2.cloned.1.call-done = f32[36,2048]{1,0:T(8,128)} async-done(((f32[36,2048]{1,0:T(8,128)}), f32[36,2048]{1,0:T(8,128)}) %all-reduce.2.cloned.1.call-update) | async-done | bytes 294928 | tf_op jit(solution)/shard_map/psum | solution.py:70
  336.8 1.4 fusion.31
  338.7 2.0 convolution_subtract_fusion
  (51 shorter events, 4.9 us)
Async XLA Ops:
  6.5 69.2 %copy-start = (f32[3,2048]{1,0:T(4,128)S(1)}, f32[3,2048]{1,0:T(4,128)}, u32[]{:S(2)}) copy-start(f32[3,2048]{1,0:T(4,128)} %param.7) | copy-start | bytes 73732
  6.5 330.3 %all-reduce.2.cloned.1.call-start = ((), (), s32[]{:S(2)}) async-start(), calls=%async_computation | async-start | bytes 655360 | tf_op jit(solution)/shard_map/psum | solution.py:70
  7.4 13.0 %collective-permute-start = (f32[1,2048]{1,0:T(1,128)S(1)}, f32[1,2048]{1,0:T(1,128)S(1)}, u32[]{:S(2)}, u32[]{:S(2)}) collective-permute-start(f32[1,2048]{1,0:T(1,128)S(1)} %slice.120), channel_id=1, source_target_pairs={{15,0},{0,1},{1,2},{2,3},{3,4},{4,5},{5,6},{6,7},{7,8},{8,9},{9,10... | collective-permute-start | bytes 24584 | tf_op jit(solution)/shard_map/ppermute | solution.py:12
  20.4 9.5 %copy-start.1 = (s32[128,2048]{1,0:T(8,128)S(1)}, s32[128,2048]{1,0:T(8,128)}, u32[]{:S(2)}) copy-start(s32[128,2048]{1,0:T(8,128)} %param.5) | copy-start | bytes 3145732
  23.1 6.8 %collective-permute-start.1 = (f32[2,2048]{1,0:T(2,128)S(1)}, f32[2,2048]{1,0:T(2,128)S(1)}, u32[]{:S(2)}, u32[]{:S(2)}) collective-permute-start(f32[2,2048]{1,0:T(2,128)S(1)} %slice.154), channel_id=1, source_target_pairs={{15,0},{0,1},{1,2},{2,3},{3,4},{4,5},{5,6},{6,7},{7,8},{8,9},{9,10... | collective-permute-start | bytes 49160 | tf_op jit(solution)/shard_map/ppermute | solution.py:12
  31.2 7.0 %collective-permute-start.2 = (f32[4,2048]{1,0:T(4,128)S(1)}, f32[4,2048]{1,0:T(4,128)S(1)}, u32[]{:S(2)}, u32[]{:S(2)}) collective-permute-start(f32[4,2048]{1,0:T(4,128)S(1)} %slice.156), channel_id=1, source_target_pairs={{15,0},{0,1},{1,2},{2,3},{3,4},{4,5},{5,6},{6,7},{7,8},{8,9},{9,10... | collective-permute-start | bytes 98312 | tf_op jit(solution)/shard_map/ppermute | solution.py:12
  39.5 7.4 %collective-permute-start.3 = (f32[8,2048]{1,0:T(8,128)S(1)}, f32[8,2048]{1,0:T(8,128)S(1)}, u32[]{:S(2)}, u32[]{:S(2)}) collective-permute-start(f32[8,2048]{1,0:T(8,128)S(1)} %slice.158), channel_id=1, source_target_pairs={{15,0},{0,1},{1,2},{2,3},{3,4},{4,5},{5,6},{6,7},{7,8},{8,9},{9,10... | collective-permute-start | bytes 196616 | tf_op jit(solution)/shard_map/ppermute | solution.py:12
  48.1 7.6 %collective-permute-start.4 = (f32[2,8,2048]{2,1,0:T(8,128)S(1)}, f32[2,8,2048]{2,1,0:T(8,128)S(1)}, u32[]{:S(2)}, u32[]{:S(2)}) collective-permute-start(f32[2,8,2048]{2,1,0:T(8,128)S(1)} %pad_maximum_fusion.4), channel_id=1, source_target_pairs={{1,0},{2,1},{3,2},{4,3},{5,4},{6,5},{7,6},{8,7},{9,8},{10,9},{11,1... | collective-permute-start | bytes 393224 | tf_op jit(solution)/shard_map/ppermute | solution.py:12
  56.1 6.2 %collective-permute-start.5 = (f32[2,4,2048]{2,1,0:T(4,128)S(1)}, f32[2,4,2048]{2,1,0:T(4,128)S(1)}, u32[]{:S(2)}, u32[]{:S(2)}) collective-permute-start(f32[2,4,2048]{2,1,0:T(4,128)S(1)} %pad_maximum_fusion.5), channel_id=1, source_target_pairs={{1,0},{2,1},{3,2},{4,3},{5,4},{6,5},{7,6},{8,7},{9,8},{10,9},{11,1... | collective-permute-start | bytes 196616 | tf_op jit(solution)/shard_map/ppermute | solution.py:12
  62.6 5.8 %collective-permute-start.6 = (f32[2,2,2048]{2,1,0:T(2,128)S(1)}, f32[2,2,2048]{2,1,0:T(2,128)S(1)}, u32[]{:S(2)}, u32[]{:S(2)}) collective-permute-start(f32[2,2,2048]{2,1,0:T(2,128)S(1)} %pad_maximum_fusion.6), channel_id=1, source_target_pairs={{1,0},{2,1},{3,2},{4,3},{5,4},{6,5},{7,6},{8,7},{9,8},{10,9},{11,1... | collective-permute-start | bytes 98312 | tf_op jit(solution)/shard_map/ppermute | solution.py:12
  68.8 6.6 %collective-permute-start.7 = (f32[2,1,2048]{2,1,0:T(1,128)S(1)}, f32[2,1,2048]{2,1,0:T(1,128)S(1)}, u32[]{:S(2)}, u32[]{:S(2)}) collective-permute-start(f32[2,1,2048]{2,1,0:T(1,128)S(1)} %pad_maximum_fusion.7), channel_id=1, source_target_pairs={{1,0},{2,1},{3,2},{4,3},{5,4},{6,5},{7,6},{8,7},{9,8},{10,9},{11,1... | collective-permute-start | bytes 49160 | tf_op jit(solution)/shard_map/ppermute | solution.py:12
  76.7 57.6 %copy-start.2 = (f32[128,6]{0,1:T(8,128)S(1)}, f32[128,6]{0,1:T(8,128)}, u32[]{:S(2)}) copy-start(f32[128,6]{0,1:T(8,128)} %param.6) | copy-start | bytes 9220
  134.4 2.6 collective-permute-start.8
Sparse Core Ops, SparseCore 0:
  201.6 135.1 all-reduce.1
where the time goes:
time: 348 us
  waiting for transfers between devices  169 us (49%)
  blocking collectives  117 us (34%)
  starting transfers between devices  24.4 us (7%)
  other arithmetic  15.3 us (4%)
  between operations  13.7 us (4%)
  matrix products  6.32 us (2%)
    psum x1, waiting for transfers between devices, local(): gram_matrix, cross_products = lax.psum((gram_matrix, cross_products), 'tm')  131 us
    psum x1, blocking collectives, local(): gram_matrix, cross_products = lax.psum((gram_matrix, cross_products), 'tm')  58.9 us
    psum x1, blocking collectives, local(): numer = lax.psum(numer, 'vox')  57.6 us
    ppermute x8, waiting for transfers between devices, from_behind(): return lax.ppermute(block, axis, route)  36.3 us
    ppermute x8, starting transfers between devices, from_behind(): return lax.ppermute(block, axis, route)  23.1 us
  transfers between devices with their start and end apart: 10, of which 10 were waited for; matrix products, arithmetic and copies ran while one was open for 1% of the time, Pallas kernels for 0%

commit v1 on v0

--- a/solution.py
+++ b/solution.py
@@ -50,7 +50,7 @@
 def local(series, spikes, motion, tissue):
     spike_free_series = despike_levelwise(series, spikes)
     numer = precise_product(spike_free_series, tissue.T)
-    numer = lax.psum(numer, "vox")
+    numer = jax.lax.all_gather(numer, "vox").sum(axis=0)
     voxel_signals = numer / float(tissue.shape[1] * lax.axis_size("vox"))
     base_regressors = jnp.concatenate([motion, voxel_signals], axis=1)
     previous_frames = shifted(base_regressors[base_regressors.shape[0] - 1 :], "tm", 1)

time: 348 us -> 314 us (0.902)
  blocking collectives: 117 us -> 83.2 us
    psum x1 -> x0, blocking collectives: 57.6 us -> none  [local(): numer = lax.psum(numer, 'vox')]
    all_gather x0 -> x1, blocking collectives: none -> 24.2 us  [local(): numer = jax.lax.all_gather(numer, 'vox').sum(axis=0)]
  transfers between devices with their start and end apart: 10 -> 10, of which waited for: 10 -> 10; matrix products, arithmetic and copies ran while one was open for 1% -> 2% of each run, Pallas kernels for 0% -> 0%
where the time goes in v1:
time: 314 us; the launch traced here: 313 us
  waiting for transfers between devices  167 us (53%)
  blocking collectives  83.2 us (26%)
  starting transfers between devices  24.4 us (8%)
  other arithmetic  15.3 us (5%)
  between operations  13.7 us (4%)
  matrix products  6.32 us (2%)
    psum x1, waiting for transfers between devices, local(): gram_matrix, cross_products = lax.psum((gram_matrix, cross_products), 'tm')  130 us
    psum x1, blocking collectives, local(): gram_matrix, cross_products = lax.psum((gram_matrix, cross_products), 'tm')  58.9 us
    ppermute x8, waiting for transfers between devices, from_behind(): return lax.ppermute(block, axis, route)  36.3 us
    all_gather x1, blocking collectives, local(): numer = jax.lax.all_gather(numer, 'vox').sum(axis=0)  24.2 us
    ppermute x8, starting transfers between devices, from_behind(): return lax.ppermute(block, axis, route)  23.1 us
    mul x4, other arithmetic, despike_levelwise(): kept_list.append(detail * keep_level(spikes, level))  6.35 us
  transfers between devices with their start and end apart: 10, of which 10 were waited for; matrix products, arithmetic and copies ran while one was open for 2% of the time, Pallas kernels for 0%

profile of v1, /device:TPU:2, one launch (start us, length us, event | category | flops | bytes accessed | tf_op | source)
XLA Modules:
  0.0 313.1 jit_solution(13603526001401679264)
XLA Ops:
  6.5 0.9 slice.120
  7.4 3.8 %collective-permute-start = (f32[1,2048]{1,0:T(1,128)S(1)}, f32[1,2048]{1,0:T(1,128)S(1)}, u32[]{:S(2)}, u32[]{:S(2)}) collective-permute-start(f32[1,2048]{1,0:T(1,128)S(1)} %slice.120), channel_id=1, source_target_pairs={{15,0},{0,1},{1,2},{2,3},{3,4},{4,5},{5,6},{6,7},{7,8},{8,9},{9,10... | collective-permute-start | bytes 24584 | tf_op jit(solution)/shard_map/ppermute | solution.py:12
  11.2 9.2 %collective-permute-done = f32[1,2048]{1,0:T(1,128)S(1)} collective-permute-done((f32[1,2048]{1,0:T(1,128)S(1)}, f32[1,2048]{1,0:T(1,128)S(1)}, u32[]{:S(2)}, u32[]{:S(2)}) %collective-permute-start) | collective-permute-done | bytes 8224 | tf_op jit(solution)/shard_map/ppermute | solution.py:12
  20.4 2.6 fusion.16
  23.1 1.9 collective-permute-start.1
  25.0 4.9 %collective-permute-done.1 = f32[2,2048]{1,0:T(2,128)S(1)} collective-permute-done((f32[2,2048]{1,0:T(2,128)S(1)}, f32[2,2048]{1,0:T(2,128)S(1)}, u32[]{:S(2)}, u32[]{:S(2)}) %collective-permute-start.1) | collective-permute-done | bytes 16416 | tf_op jit(solution)/shard_map/ppermute | solution.py:12
  29.9 1.3 fusion.13
  31.2 1.9 collective-permute-start.2
  33.1 5.1 %collective-permute-done.2 = f32[4,2048]{1,0:T(4,128)S(1)} collective-permute-done((f32[4,2048]{1,0:T(4,128)S(1)}, f32[4,2048]{1,0:T(4,128)S(1)}, u32[]{:S(2)}, u32[]{:S(2)}) %collective-permute-start.2) | collective-permute-done | bytes 32800 | tf_op jit(solution)/shard_map/ppermute | solution.py:12
  38.2 1.3 fusion.9
  39.5 1.9 collective-permute-start.3
  41.5 5.3 %collective-permute-done.3 = f32[8,2048]{1,0:T(8,128)S(1)} collective-permute-done((f32[8,2048]{1,0:T(8,128)S(1)}, f32[8,2048]{1,0:T(8,128)S(1)}, u32[]{:S(2)}, u32[]{:S(2)}) %collective-permute-start.3) | collective-permute-done | bytes 65568 | tf_op jit(solution)/shard_map/ppermute | solution.py:12
  46.9 1.2 fusion.4
  48.1 1.9 collective-permute-start.4
  50.2 5.4 %collective-permute-done.4 = f32[2,8,2048]{2,1,0:T(8,128)S(1)} collective-permute-done((f32[2,8,2048]{2,1,0:T(8,128)S(1)}, f32[2,8,2048]{2,1,0:T(8,128)S(1)}, u32[]{:S(2)}, u32[]{:S(2)}) %collective-permute-start.4) | collective-permute-done | bytes 131104 | tf_op jit(solution)/shard_map/ppermute | solution.py:12
  56.1 2.4 collective-permute-start.5
  58.7 3.5 %collective-permute-done.5 = f32[2,4,2048]{2,1,0:T(4,128)S(1)} collective-permute-done((f32[2,4,2048]{2,1,0:T(4,128)S(1)}, f32[2,4,2048]{2,1,0:T(4,128)S(1)}, u32[]{:S(2)}, u32[]{:S(2)}) %collective-permute-start.5) | collective-permute-done | bytes 65568 | tf_op jit(solution)/shard_map/ppermute | solution.py:12
  62.6 4.0 %collective-permute-start.6 = (f32[2,2,2048]{2,1,0:T(2,128)S(1)}, f32[2,2,2048]{2,1,0:T(2,128)S(1)}, u32[]{:S(2)}, u32[]{:S(2)}) collective-permute-start(f32[2,2,2048]{2,1,0:T(2,128)S(1)} %pad_maximum_fusion.6), channel_id=1, source_target_pairs={{1,0},{2,1},{3,2},{4,3},{5,4},{6,5},{7,6},{8,7},{9,8},{10,9},{11,1... | collective-permute-start | bytes 98312 | tf_op jit(solution)/shard_map/ppermute | solution.py:12
  66.8 1.6 collective-permute-done.6
  68.8 5.2 %collective-permute-start.7 = (f32[2,1,2048]{2,1,0:T(1,128)S(1)}, f32[2,1,2048]{2,1,0:T(1,128)S(1)}, u32[]{:S(2)}, u32[]{:S(2)}) collective-permute-start(f32[2,1,2048]{2,1,0:T(1,128)S(1)} %pad_maximum_fusion.7), channel_id=1, source_target_pairs={{1,0},{2,1},{3,2},{4,3},{5,4},{6,5},{7,6},{8,7},{9,8},{10,9},{11,1... | collective-permute-start | bytes 49160 | tf_op jit(solution)/shard_map/ppermute | solution.py:12
  74.2 1.2 collective-permute-done.7
  75.8 0.9 fusion.38
  76.7 24.2 %all-gather = f32[4096,3]{0,1:T(4,128)S(1)} all-gather(f32[128,3]{0,1:T(4,128)S(1)} %fusion.38), channel_id=2, replica_groups=mesh['vox'=32,'tm'=16] {'vox'}, dimensions={0}, use_global_device_ids=true | all-gather | bytes 50688 | tf_op jit(solution)/shard_map/all_gather | solution.py:53
  101.7 1.3 collective-permute-start.8
  103.0 1.3 collective-permute-done.8
  105.1 1.4 fusion.40
  106.4 58.9 %psum.14 = f32[36,36]{0,1:T(8,128)S(1)} all-reduce(f32[36,36]{0,1:T(8,128)S(1)} %fusion.39), channel_id=1, replica_groups=mesh['vox'=32,'tm'=16] {'tm'}, use_global_device_ids=true, to_apply=%region_1.2 | all-reduce | flops 1296 | bytes 10368 | tf_op jit(solution)/shard_map/psum | solution.py:70
  165.5 3.3 %cholesky.16 = f32[36,36]{1,0:T(8,128)S(1)} custom-call(f32[36,36]{1,0:T(8,128)S(1)} %fusion.33), custom_call_target="Cholesky" | custom-call | tf_op jit(solution)/shard_map/jit(cholesky)/cholesky | solution.py:71
  170.1 2.8 custom-call.10
  172.8 129.5 %all-reduce.2.cloned.1.call-done = f32[36,2048]{1,0:T(8,128)} async-done(((f32[36,2048]{1,0:T(8,128)}), f32[36,2048]{1,0:T(8,128)}) %all-reduce.2.cloned.1.call-update) | async-done | bytes 294928 | tf_op jit(solution)/shard_map/psum | solution.py:70
  302.4 1.4 fusion.31
  304.3 2.0 convolution_subtract_fusion
  (52 shorter events, 5.6 us)
Async XLA Ops:
  6.5 69.2 %copy-start = (f32[3,2048]{1,0:T(4,128)S(1)}, f32[3,2048]{1,0:T(4,128)}, u32[]{:S(2)}) copy-start(f32[3,2048]{1,0:T(4,128)} %param.7) | copy-start | bytes 73732
  6.5 295.9 %all-reduce.2.cloned.1.call-start = ((), (), s32[]{:S(2)}) async-start(), calls=%async_computation | async-start | bytes 655360 | tf_op jit(solution)/shard_map/psum | solution.py:70
  7.4 13.0 %collective-permute-start = (f32[1,2048]{1,0:T(1,128)S(1)}, f32[1,2048]{1,0:T(1,128)S(1)}, u32[]{:S(2)}, u32[]{:S(2)}) collective-permute-start(f32[1,2048]{1,0:T(1,128)S(1)} %slice.120), channel_id=1, source_target_pairs={{15,0},{0,1},{1,2},{2,3},{3,4},{4,5},{5,6},{6,7},{7,8},{8,9},{9,10... | collective-permute-start | bytes 24584 | tf_op jit(solution)/shard_map/ppermute | solution.py:12
  20.4 9.5 %copy-start.1 = (s32[128,2048]{1,0:T(8,128)S(1)}, s32[128,2048]{1,0:T(8,128)}, u32[]{:S(2)}) copy-start(s32[128,2048]{1,0:T(8,128)} %param.5) | copy-start | bytes 3145732
  23.1 6.8 %collective-permute-start.1 = (f32[2,2048]{1,0:T(2,128)S(1)}, f32[2,2048]{1,0:T(2,128)S(1)}, u32[]{:S(2)}, u32[]{:S(2)}) collective-permute-start(f32[2,2048]{1,0:T(2,128)S(1)} %slice.154), channel_id=1, source_target_pairs={{15,0},{0,1},{1,2},{2,3},{3,4},{4,5},{5,6},{6,7},{7,8},{8,9},{9,10... | collective-permute-start | bytes 49160 | tf_op jit(solution)/shard_map/ppermute | solution.py:12
  31.2 7.0 %collective-permute-start.2 = (f32[4,2048]{1,0:T(4,128)S(1)}, f32[4,2048]{1,0:T(4,128)S(1)}, u32[]{:S(2)}, u32[]{:S(2)}) collective-permute-start(f32[4,2048]{1,0:T(4,128)S(1)} %slice.156), channel_id=1, source_target_pairs={{15,0},{0,1},{1,2},{2,3},{3,4},{4,5},{5,6},{6,7},{7,8},{8,9},{9,10... | collective-permute-start | bytes 98312 | tf_op jit(solution)/shard_map/ppermute | solution.py:12
  39.5 7.4 %collective-permute-start.3 = (f32[8,2048]{1,0:T(8,128)S(1)}, f32[8,2048]{1,0:T(8,128)S(1)}, u32[]{:S(2)}, u32[]{:S(2)}) collective-permute-start(f32[8,2048]{1,0:T(8,128)S(1)} %slice.158), channel_id=1, source_target_pairs={{15,0},{0,1},{1,2},{2,3},{3,4},{4,5},{5,6},{6,7},{7,8},{8,9},{9,10... | collective-permute-start | bytes 196616 | tf_op jit(solution)/shard_map/ppermute | solution.py:12
  48.1 7.6 %collective-permute-start.4 = (f32[2,8,2048]{2,1,0:T(8,128)S(1)}, f32[2,8,2048]{2,1,0:T(8,128)S(1)}, u32[]{:S(2)}, u32[]{:S(2)}) collective-permute-start(f32[2,8,2048]{2,1,0:T(8,128)S(1)} %pad_maximum_fusion.4), channel_id=1, source_target_pairs={{1,0},{2,1},{3,2},{4,3},{5,4},{6,5},{7,6},{8,7},{9,8},{10,9},{11,1... | collective-permute-start | bytes 393224 | tf_op jit(solution)/shard_map/ppermute | solution.py:12
  56.1 6.2 %collective-permute-start.5 = (f32[2,4,2048]{2,1,0:T(4,128)S(1)}, f32[2,4,2048]{2,1,0:T(4,128)S(1)}, u32[]{:S(2)}, u32[]{:S(2)}) collective-permute-start(f32[2,4,2048]{2,1,0:T(4,128)S(1)} %pad_maximum_fusion.5), channel_id=1, source_target_pairs={{1,0},{2,1},{3,2},{4,3},{5,4},{6,5},{7,6},{8,7},{9,8},{10,9},{11,1... | collective-permute-start | bytes 196616 | tf_op jit(solution)/shard_map/ppermute | solution.py:12
  62.6 5.8 %collective-permute-start.6 = (f32[2,2,2048]{2,1,0:T(2,128)S(1)}, f32[2,2,2048]{2,1,0:T(2,128)S(1)}, u32[]{:S(2)}, u32[]{:S(2)}) collective-permute-start(f32[2,2,2048]{2,1,0:T(2,128)S(1)} %pad_maximum_fusion.6), channel_id=1, source_target_pairs={{1,0},{2,1},{3,2},{4,3},{5,4},{6,5},{7,6},{8,7},{9,8},{10,9},{11,1... | collective-permute-start | bytes 98312 | tf_op jit(solution)/shard_map/ppermute | solution.py:12
  68.8 6.6 %collective-permute-start.7 = (f32[2,1,2048]{2,1,0:T(1,128)S(1)}, f32[2,1,2048]{2,1,0:T(1,128)S(1)}, u32[]{:S(2)}, u32[]{:S(2)}) collective-permute-start(f32[2,1,2048]{2,1,0:T(1,128)S(1)} %pad_maximum_fusion.7), channel_id=1, source_target_pairs={{1,0},{2,1},{3,2},{4,3},{5,4},{6,5},{7,6},{8,7},{9,8},{10,9},{11,1... | collective-permute-start | bytes 49160 | tf_op jit(solution)/shard_map/ppermute | solution.py:12
  101.0 0.7 copy-start.2
  101.7 2.6 collective-permute-start.8
Sparse Core Ops, SparseCore 0:
  168.9 133.4 all-reduce.1
